TPU v7x, 128 devices: a whole 4x4x4 slice. The times are simulated.
128 devices in a mesh: expert: 16 (over z, x), dp: 8 (over y, core).
Axes of the slice: x: 4, y: 4, z: 4, core: 2. Of those that a mesh axis runs over, the one named last changes fastest.
Arguments:
- tokens: bfloat16 [16, 480, 7168], P('expert', 'dp'), may hold values from -6 to 6
- cotangent: bfloat16 [16, 480, 7168], P('expert', 'dp'), may hold values from -1.5 to 1.5
- counts: int32 [16, 8], replicated, may hold values from 1 to 60, as said below
- w_gate: bfloat16 [16, 7168, 2048], P('expert', None, 'dp'), may hold values from -0.0625 to 0.0625
- w_up: bfloat16 [16, 7168, 2048], P('expert', None, 'dp'), may hold values from -0.0625 to 0.0625
- w_down: bfloat16 [16, 2048, 7168], P('expert', 'dp'), may hold values from -0.125 to 0.125
Outputs:
- outputs: bfloat16 [16, 480, 7168], P('expert', 'dp')
- input_grads: bfloat16 [16, 480, 7168], P('expert', 'dp')
- gate_grad: bfloat16 [16, 7168, 2048], P('expert', None, 'dp')
- up_grad: bfloat16 [16, 7168, 2048], P('expert', None, 'dp')
- down_grad: bfloat16 [16, 2048, 7168], P('expert', 'dp')
Inputs may be any that keep to these rules, and one draw needn't show every extreme that they name: For each expert e below 8, exactly one of experts e and e + 8 is hot: all its counts exceed 40 - 20 and one equals 60; every count of the other is at most 20 and one equals 20.
All inputs are finite; a program needn't handle non-finite values.
Results may differ from a plain program's by a relative error of at most 0.012.
Values may be sent and summed in bfloat16 or wider, within the bound.
No kernel may reach another device: no remote copies, remote signals or barrier semaphores. Data moves between devices by JAX's collectives and lax.ppermute only.
A program may use at most 192 MiB of HBM per device.

v0:
```python
import jax
import jax.numpy as jnp
from jax import lax
from jax.sharding import PartitionSpec as P


def silu_slope(value):
    sigma = jax.nn.sigmoid(value)
    return sigma * (1.0 + value * (1.0 - sigma))


def contract_last(left, right):
    return lax.dot_general(
        left, right, (((1,), (1,)), ((), ())), preferred_element_type=jnp.float32
    )


def contract_first(left, right):
    return lax.dot_general(
        left, right, (((0,), (0,)), ((), ())), preferred_element_type=jnp.float32
    )


def expert_work(rows, cot_rows, gate_w, up_w, down_w):
    gate = jnp.dot(rows, gate_w, preferred_element_type=jnp.float32)
    up = jnp.dot(rows, up_w, preferred_element_type=jnp.float32)
    active = jax.nn.silu(gate)
    hidden = (active * up).astype(jnp.bfloat16)
    out_part = jnp.dot(hidden, down_w, preferred_element_type=jnp.float32).astype(jnp.bfloat16)
    out_part, hidden, gate, up = lax.optimization_barrier((out_part, hidden, gate, up))
    active = jax.nn.silu(gate)
    hidden_grad = contract_last(cot_rows, down_w)
    gate_act = (hidden_grad * up * silu_slope(gate)).astype(jnp.bfloat16)
    up_act = (hidden_grad * active).astype(jnp.bfloat16)
    in_part = contract_last(gate_act, gate_w) + contract_last(up_act, up_w)
    gate_term = contract_first(rows, gate_act)
    up_term = contract_first(rows, up_act)
    down_term = contract_first(hidden, cot_rows)
    return (out_part, in_part, gate_term, up_term, down_term)


def shards(tokens, cotangent, counts, w_gate, w_up, w_down):
    rows_in = tokens[0]
    cot_in = cotangent[0]
    gate_w = w_gate[0]
    up_w = w_up[0]
    down_w = w_down[0]
    expert_pos = lax.axis_index("expert")
    batch_pos = lax.axis_index("dp")
    expert_ids = jnp.arange(counts.shape[0], dtype=jnp.int32)
    batch_ids = jnp.arange(counts.shape[1], dtype=jnp.int32)
    own_counts = jnp.sum(jnp.where(expert_ids[:, None] == expert_pos, counts, 0), axis=0)
    own_total = jnp.sum(jnp.where(batch_ids == batch_pos, own_counts, 0))
    slots = rows_in.shape[0]
    valid = (jnp.arange(slots, dtype=jnp.int32) < own_total)[:, None]
    masked = jnp.where(valid, rows_in, jnp.zeros_like(rows_in))
    masked_cot = jnp.where(valid, cot_in, jnp.zeros_like(cot_in))
    all_rows = lax.all_gather(masked, "dp", axis=0, tiled=True)
    all_cot = lax.all_gather(masked_cot, "dp", axis=0, tiled=True)
    out_part, in_part, gate_term, up_term, down_term = expert_work(
        all_rows, all_cot, gate_w, up_w, down_w
    )
    groups = lax.axis_size("dp")
    outputs = lax.psum_scatter(
        out_part.reshape(groups, slots, -1), "dp", scatter_dimension=0, tiled=False
    )
    input_grads = lax.psum_scatter(
        in_part.astype(jnp.bfloat16).reshape(groups, slots, -1),
        "dp",
        scatter_dimension=0,
        tiled=False,
    )
    gate_grad = gate_term.astype(jnp.bfloat16)
    up_grad = up_term.astype(jnp.bfloat16)
    down_grad = down_term.astype(jnp.bfloat16)
    return (outputs[None], input_grads[None], gate_grad[None], up_grad[None], down_grad[None])


def solution(mesh):
    placed = (
        P("expert", "dp", None),
        P("expert", "dp", None),
        P(),
        P("expert", None, "dp"),
        P("expert", None, "dp"),
        P("expert", "dp", None),
    )
    return jax.shard_map(
        shards,
        mesh=mesh,
        in_specs=placed,
        out_specs=(
            P("expert", "dp", None),
            P("expert", "dp", None),
            P("expert", None, "dp"),
            P("expert", None, "dp"),
            P("expert", "dp", None),
        ),
        check_vma=False,
    )
```

profile of v0, /device:TPU:1, one launch (start us, length us, event | category | flops | bytes accessed | tf_op | source)
XLA Modules:
  0.0 215.1 jit_solution(16203403560469040614)
XLA Ops:
  7.2 0.0 all-gather.5.cloned.1.call-start
  7.2 0.8 select_reduce_fusion
  8.0 0.6 fusion.15
  8.7 0.6 iota_compare_fusion.1
  9.3 2.9 %fusion.13 = (bf16[1,60,7168]{2,1,0:T(8,128)(2,1)}, bf16[1,60,7168]{2,1,0:T(8,128)(2,1)}) fusion(bf16[1,60,7168]{2,1,0:T(8,128)(2,1)} %param.7, pred[60]{0:T(512)(128)(4,1)S(1)} %iota_compare_fusion.1, bf16[1,60,7168]{2,1,0:T(8,128)(2,1)} %param.6), kind=kLoop, calls=%fused_computation.19 | loop fusion | flops 860160 | bytes 3440700
  12.2 0.0 all-gather.5.cloned.1.call-update
  12.2 0.0 all-gather.7.cloned.1.call-start
  12.3 0.7 all-gather.7.cloned.1.call-update
  13.0 0.0 reduce-scatter.3.cloned.1.call-start
  13.0 48.2 %all-gather.5.cloned.1.call-done = bf16[8,60,7168]{2,1,0:T(8,128)(2,1)} async-done(((bf16[1,60,7168]{2,1,0:T(8,128)(2,1)}), bf16[8,60,7168]{2,1,0:T(8,128)(2,1)}) %all-gather.5.cloned.1.call-update) | async-done | bytes 6881296 | tf_op jit(solution)/shard_map/all_gather | solution.py:58
  61.3 6.9 %reshape.28 = bf16[480,7168]{1,0:T(8,128)(2,1)} reshape(bf16[8,60,7168]{2,1,0:T(8,128)(2,1)} %all-gather.5.cloned.1.call-done) | data formatting | bytes 13762560
  68.2 0.0 copy-start
  68.2 0.0 copy-start.1
  68.2 6.2 %fusion.11 = f32[480,256]{1,0:T(8,128)S(1)} fusion(bf16[480,7168]{1,0:T(8,128)(2,1)} %reshape.28, bf16[1,7168,256]{2,1,0:T(8,128)(2,1)} %param.9), kind=kOutput, calls=%fused_computation.16 | convolution fusion | flops 1761607680 | bytes 11042816 | tf_op jit(solution)/shard_map/dot_general | solution.py:25
  74.3 0.4 copy-done
  74.8 1.6 copy-done.1
  76.4 0.0 copy-start.3
  76.4 1.9 multiply_convert_fusion.2
  78.4 0.1 copy-done.3
  78.4 4.8 %convolution_convert_fusion = bf16[480,7168]{1,0:T(8,128)(2,1)} fusion(bf16[480,256]{1,0:T(8,128)(2,1)S(1)} %get-tuple-element.12, bf16[1,256,7168]{2,1,0:T(8,128)(2,1)S(1)} %copy-done.3), kind=kOutput, calls=%fused_computation.1 | convolution fusion | flops 1765048320 | bytes 10797056 | tf_op jit(solution)/shard_map/dot_general | solution.py:29
  83.2 6.9 %reshape.25 = bf16[8,60,7168]{2,1,0:T(8,128)(2,1)} reshape(bf16[480,7168]{1,0:T(8,128)(2,1)} %convolution_convert_fusion) | data formatting | bytes 13762560 | tf_op jit(solution)/shard_map/reshape | solution.py:65
  90.1 0.0 reduce-scatter.3.cloned.1.call-update
  90.2 0.2 reduce-scatter.5.cloned.1.call-start
  90.4 18.5 %all-gather.7.cloned.1.call-done = bf16[8,60,7168]{2,1,0:T(8,128)(2,1)} async-done(((bf16[1,60,7168]{2,1,0:T(8,128)(2,1)}), bf16[8,60,7168]{2,1,0:T(8,128)(2,1)}) %all-gather.7.cloned.1.call-update) | async-done | bytes 6881296 | tf_op jit(solution)/shard_map/all_gather | solution.py:59
  108.9 6.8 %reshape.30 = bf16[480,7168]{1,0:T(8,128)(2,1)} reshape(bf16[8,60,7168]{2,1,0:T(8,128)(2,1)} %all-gather.7.cloned.1.call-done) | data formatting | bytes 13762560
  115.7 0.0 copy-start.4
  115.7 6.2 %multiply_convert_fusion = (bf16[480,256]{1,0:T(8,128)(2,1)S(1)}, bf16[480,256]{1,0:T(8,128)(2,1)S(1)}) fusion(f32[480,256]{1,0:T(8,128)S(1)} %fusion.11, f32[480,256]{1,0:T(8,128)S(1)} %get-tuple-element.10, bf16[480,7168]{1,0:T(8,128)(2,1)} %reshape.30, bf16[1,256,7168]{2,1,0:T(8,128)(2,1)} %param.11), kind=kOutput, calls=%fused_computation.22 | convolution fusion | flops 1763205120 | bytes 12025856 | tf_op jit(solution)/shard_map/dot_general | solution.py:13
  121.9 0.0 copy-done.4
  121.9 0.0 copy-start.2
  121.9 6.9 %fusion.9 = f32[480,7168]{1,0:T(8,128)} fusion(bf16[480,256]{1,0:T(8,128)(2,1)S(1)} %get-tuple-element.14, bf16[1,7168,256]{2,1,0:T(8,128)(2,1)S(1)} %copy-done.4), kind=kOutput, calls=%fused_computation.14 | convolution fusion | flops 1761607680 | bytes 17678336 | tf_op jit(solution)/shard_map/dot_general | solution.py:13
  128.8 0.0 copy-done.2
  128.8 10.0 %add_convert_fusion = bf16[480,7168]{1,0:T(8,128)(2,1)} fusion(f32[480,7168]{1,0:T(8,128)} %fusion.9, bf16[480,256]{1,0:T(8,128)(2,1)S(1)} %get-tuple-element.13, bf16[1,7168,256]{2,1,0:T(8,128)(2,1)S(1)} %copy-done.2), kind=kOutput, calls=%fused_computation | convolution fusion | flops 1768488960 | bytes 24559616 | tf_op jit(solution)/shard_map/dot_general | solution.py:13
  138.9 7.0 %reshape.26 = bf16[8,60,7168]{2,1,0:T(8,128)(2,1)} reshape(bf16[480,7168]{1,0:T(8,128)(2,1)} %add_convert_fusion) | data formatting | bytes 13762560 | tf_op jit(solution)/shard_map/reshape | solution.py:68
  145.8 0.0 slice-start
  145.8 0.0 reduce-scatter.5.cloned.1.call-update
  145.9 0.0 slice-start.1
  145.9 7.2 %fusion.2 = bf16[1,256,7168]{2,1,0:T(8,128)(2,1)} fusion(bf16[480,256]{1,0:T(8,128)(2,1)S(1)} %get-tuple-element.12, bf16[480,7168]{1,0:T(8,128)(2,1)} %reshape.30), kind=kOutput, calls=%fused_computation.7 | convolution fusion | flops 1763442688 | bytes 10797056 | tf_op jit(solution)/shard_map/dot_general | solution.py:19
  153.1 0.0 slice-done
  153.1 0.0 slice-done.1
  153.1 4.0 %fusion.1 = bf16[1,7168,256]{2,1,0:T(8,128)(2,1)} fusion(bf16[480,7168]{1,0:T(8,128)(2,1)S(1)} %bitcast.50, bf16[480,256]{1,0:T(8,128)(2,1)S(1)} %get-tuple-element.13), kind=kOutput, calls=%fused_computation.6 | convolution fusion | flops 1763442688 | bytes 10797056 | tf_op jit(solution)/shard_map/dot_general | solution.py:19
  157.1 4.0 %fusion = bf16[1,7168,256]{2,1,0:T(8,128)(2,1)} fusion(bf16[480,7168]{1,0:T(8,128)(2,1)S(1)} %bitcast.50, bf16[480,256]{1,0:T(8,128)(2,1)S(1)} %get-tuple-element.14), kind=kOutput, calls=%fused_computation.5 | convolution fusion | flops 1763442688 | bytes 10797056 | tf_op jit(solution)/shard_map/dot_general | solution.py:19
  161.1 0.0 reduce-scatter.3.cloned.1.call-done
  161.1 47.4 %reduce-scatter.5.cloned.1.call-done = bf16[1,60,7168]{2,1,0:T(8,128)(2,1)} async-done(((bf16[8,60,7168]{2,1,0:T(8,128)(2,1)}), bf16[1,60,7168]{2,1,0:T(8,128)(2,1)}) %reduce-scatter.5.cloned.1.call-update) | async-done | bytes 860176 | tf_op jit(solution)/shard_map/reduce_scatter | solution.py:67
  (2 shorter events, 0.0 us)
Async XLA Ops:
  7.2 54.1 %all-gather.5.cloned.1.call-start = ((), (), s32[]{:S(2)}) async-start(), calls=%async_computation.4 | async-start | bytes 8257536 | tf_op jit(solution)/shard_map/all_gather | solution.py:58
  12.2 96.7 %all-gather.7.cloned.1.call-start = ((), (), s32[]{:S(2)}) async-start(), calls=%async_computation.5 | async-start | bytes 8257536 | tf_op jit(solution)/shard_map/all_gather | solution.py:59
  13.0 148.2 %reduce-scatter.3.cloned.1.call-start = ((), (), s32[]{:S(2)}) async-start(), calls=%async_computation.2 | async-start | bytes 8257536 | tf_op jit(solution)/shard_map/reduce_scatter | solution.py:64
  68.2 6.6 %copy-start = (bf16[480,7168]{1,0:T(8,128)(2,1)S(1)}, bf16[480,7168]{1,0:T(8,128)(2,1)}, u32[]{:S(2)}) copy-start(bf16[480,7168]{1,0:T(8,128)(2,1)} %reshape.28) | copy-start | bytes 20643844
  68.2 8.2 %copy-start.1 = (bf16[1,7168,256]{2,1,0:T(8,128)(2,1)S(1)}, bf16[1,7168,256]{2,1,0:T(8,128)(2,1)}, u32[]{:S(2)}) copy-start(bf16[1,7168,256]{2,1,0:T(8,128)(2,1)} %param.10) | copy-start | bytes 11010052
  76.4 2.0 copy-start.3
  90.2 118.4 %reduce-scatter.5.cloned.1.call-start = ((), (), s32[]{:S(2)}) async-start(), calls=%async_computation.3 | async-start | bytes 8257536 | tf_op jit(solution)/shard_map/reduce_scatter | solution.py:67
  115.7 6.2 %copy-start.4 = (bf16[1,7168,256]{2,1,0:T(8,128)(2,1)S(1)}, bf16[1,7168,256]{2,1,0:T(8,128)(2,1)}, u32[]{:S(2)}) copy-start(bf16[1,7168,256]{2,1,0:T(8,128)(2,1)} %param.9) | copy-start | bytes 11010052
  121.9 7.0 %copy-start.2 = (bf16[1,7168,256]{2,1,0:T(8,128)(2,1)S(1)}, bf16[1,7168,256]{2,1,0:T(8,128)(2,1)}, u32[]{:S(2)}) copy-start(bf16[1,7168,256]{2,1,0:T(8,128)(2,1)} %param.10) | copy-start | bytes 11010052
  145.8 7.2 %slice-start = ((s8[6881280]{0:T(1024)(128)(4,1)}), s8[2686976]{0:T(1024)(128)(4,1)S(1)}, s32[]{:S(2)}) async-start(s8[6881280]{0:T(1024)(128)(4,1)} %bitcast.49), calls=%async_computation.6 | async-start | bytes 5373952
  145.9 7.2 %slice-start.1 = ((s8[6881280]{0:T(1024)(128)(4,1)}), s8[4194304]{0:T(1024)(128)(4,1)S(1)}, s32[]{:S(2)}) async-start(s8[6881280]{0:T(1024)(128)(4,1)} %bitcast.49), calls=%async_computation.7 | async-start | bytes 8388608
Sparse Core Ops, SparseCore 0:
  12.3 48.8 all-gather.4
  63.5 45.3 all-gather.6
  111.9 46.6 reduce-scatter.2
  161.4 47.0 reduce-scatter.4
where the time goes:
time: 215 us
  waiting for transfers between devices  115 us (53%)
  matrix products  51.3 us (24%)
  local copies, waits for them, and re-layouts  29.7 us (14%)
  between operations  13.8 us (6%)
  other arithmetic  4.97 us (2%)
    all_gather x1, waiting for transfers between devices, shards(): all_rows = lax.all_gather(masked, 'dp', axis=0, tiled=True)  48.2 us
    reduce_scatter x1, waiting for transfers between devices, shards(): lax.psum_scatter(in_part.astype(jnp.bfloat16).reshape(groups, slots, -1),...  47.4 us
    dot_general x3, matrix products, contract_last(): lax.dot_general(left, right, (((1,), (1,)), ((), ())), preferred_element_...  23.2 us
    all_gather x1, waiting for transfers between devices, shards(): all_cot = lax.all_gather(masked_cot, 'dp', axis=0, tiled=True)  18.5 us
    unnamed x16, local copies, waits for them, and re-layouts  15.9 us
    dot_general x3, matrix products, contract_first(): lax.dot_general(left, right, (((0,), (0,)), ((), ())), preferred_element_...  15.2 us
    reshape x1, local copies, waits for them, and re-layouts, shards(): in_part.astype(jnp.bfloat16).reshape(groups, slots, -1)  6.95 us
    reshape x1, local copies, waits for them, and re-layouts, shards(): out_part.reshape(groups, slots, -1)  6.9 us
  transfers between devices with their start and end apart: 4, of which 3 were waited for; matrix products, arithmetic and copies ran while one was open for 37% of the time, Pallas kernels for 0%

commit v1 on v0

--- a/solution.py
+++ b/solution.py
@@ -2,6 +2,22 @@
 import jax.numpy as jnp
 from jax import lax
 from jax.sharding import PartitionSpec as P
+
+
+def gather_around(x, axis, dim):
+    ways, here, lap = (lax.axis_size(axis), lax.axis_index(axis), x.shape[dim])
+    dims = [n * ways if d == dim else n for d, n in enumerate(x.shape)]
+    full = lax.dynamic_update_slice_in_dim(jnp.zeros(dims, x.dtype), x, here * lap, axis=dim)
+    going_up = going_down = x
+    for far in range(1, ways // 2 + 1):
+        going_up = lax.ppermute(going_up, axis, [(d, (d + 1) % ways) for d in range(ways)])
+        full = lax.dynamic_update_slice_in_dim(full, going_up, (here - far) % ways * lap, axis=dim)
+        if 2 * far < ways:
+            going_down = lax.ppermute(going_down, axis, [(d, (d - 1) % ways) for d in range(ways)])
+            full = lax.dynamic_update_slice_in_dim(
+                full, going_down, (here + far) % ways * lap, axis=dim
+            )
+    return full
 
 
 def silu_slope(value):
@@ -56,7 +72,7 @@
     masked = jnp.where(valid, rows_in, jnp.zeros_like(rows_in))
     masked_cot = jnp.where(valid, cot_in, jnp.zeros_like(cot_in))
     all_rows = lax.all_gather(masked, "dp", axis=0, tiled=True)
-    all_cot = lax.all_gather(masked_cot, "dp", axis=0, tiled=True)
+    all_cot = gather_around(masked_cot, "dp", 0)
     out_part, in_part, gate_term, up_term, down_term = expert_work(
         all_rows, all_cot, gate_w, up_w, down_w
     )

time: 215 us -> 280 us (1.30)
  local copies, waits for them, and re-layouts: 29.7 us -> 62 us
  waiting for transfers between devices: 115 us -> 132 us
  starting transfers between devices: 0.34 us -> 14.4 us
    ppermute x0 -> x7, waiting for transfers between devices: none -> 47.4 us  [the longest x4 45.8 us: gather_around(): lax.ppermute(going_up, axis, [(d, (d + 1) % ways) for d in range(ways)])]
    dynamic_update_slice x0 -> x8, local copies, waits for them, and re-layouts: none -> 36.9 us  [the longest x4 18.1 us: gather_around(): lax.dynamic_update_slice_in_dim(full, going_up, (here - far) % ways * lap...]
    all_gather x1 -> x0, waiting for transfers between devices: 18.5 us -> none  [shards(): all_cot = lax.all_gather(masked_cot, 'dp', axis=0, tiled=True)]
    ppermute x0 -> x7, starting transfers between devices: none -> 14.1 us  [the longest x4 8.05 us: gather_around(): lax.ppermute(going_up, axis, [(d, (d + 1) % ways) for d in range(ways)])]
    reduce_scatter x1, waiting for transfers between devices: 47.4 us -> 35.6 us  [shards(): lax.psum_scatter(in_part.astype(jnp.bfloat16).reshape(groups, slots, -1),...]
    unnamed x16 -> x21, local copies, waits for them, and re-layouts: 15.9 us -> 7.86 us
    broadcast_in_dim x0 -> x1, local copies, waits for them, and re-layouts: none -> 3.59 us  [gather_around(): jnp.zeros(dims, x.dtype)]
    unnamed x2 -> x1, other arithmetic: 2.87 us -> 0.01 us
  transfers between devices with their start and end apart: 4 -> 10, of which waited for: 3 -> 7; matrix products, arithmetic and copies ran while one was open for 37% -> 31% of each run, Pallas kernels for 0% -> 0%
where the time goes in v1:
time: 280 us; the launch traced here: 279 us
  waiting for transfers between devices  132 us (47%)
  local copies, waits for them, and re-layouts  62 us (22%)
  matrix products  51.6 us (18%)
  starting transfers between devices  14.4 us (5%)
  between operations  13.8 us (5%)
  other arithmetic  4.67 us (2%)
    all_gather x1, waiting for transfers between devices, shards(): all_rows = lax.all_gather(masked, 'dp', axis=0, tiled=True)  49 us
    ppermute x4, waiting for transfers between devices, gather_around(): lax.ppermute(going_up, axis, [(d, (d + 1) % ways) for d in range(ways)])  45.8 us
    reduce_scatter x1, waiting for transfers between devices, shards(): lax.psum_scatter(in_part.astype(jnp.bfloat16).reshape(groups, slots, -1),...  35.6 us
    dot_general x3, matrix products, contract_last(): lax.dot_general(left, right, (((1,), (1,)), ((), ())), preferred_element_...  22.9 us
    dynamic_update_slice x4, local copies, waits for them, and re-layouts, gather_around(): lax.dynamic_update_slice_in_dim(full, going_up, (here - far) % ways * lap...  18.1 us
    dot_general x3, matrix products, contract_first(): lax.dot_general(left, right, (((0,), (0,)), ((), ())), preferred_element_...  15.1 us
    dynamic_update_slice x3, local copies, waits for them, and re-layouts, gather_around(): lax.dynamic_update_slice_in_dim(full, going_down, (here + far) % ways * l...  14.3 us
    ppermute x4, starting transfers between devices, gather_around(): lax.ppermute(going_up, axis, [(d, (d + 1) % ways) for d in range(ways)])  8.05 us
  transfers between devices with their start and end apart: 10, of which 7 were waited for; matrix products, arithmetic and copies ran while one was open for 31% of the time, Pallas kernels for 0%

profile of v1, /device:TPU:1, one launch (start us, length us, event | category | flops | bytes accessed | tf_op | source)
XLA Modules:
  0.0 278.5 jit_solution(18351495931752930758)
XLA Ops:
  7.2 0.0 all-gather.3.cloned.1.call-start
  7.2 0.8 select_reduce_fusion
  8.0 0.6 fusion.14
  8.7 0.6 iota_compare_fusion.1
  9.3 2.6 bitcast_select_fusion
  11.9 0.0 all-gather.3.cloned.1.call-update
  11.9 0.0 reduce-scatter.3.cloned.1.call-start
  12.0 49.0 %all-gather.3.cloned.1.call-done = bf16[8,60,7168]{2,1,0:T(8,128)(2,1)} async-done(((bf16[1,60,7168]{2,1,0:T(8,128)(2,1)}), bf16[8,60,7168]{2,1,0:T(8,128)(2,1)}) %all-gather.3.cloned.1.call-update) | async-done | bytes 6881296 | tf_op jit(solution)/shard_map/all_gather | solution.py:74
  60.9 6.9 %reshape.28 = bf16[480,7168]{1,0:T(8,128)(2,1)} reshape(bf16[8,60,7168]{2,1,0:T(8,128)(2,1)} %all-gather.3.cloned.1.call-done) | data formatting | bytes 13762560
  67.9 0.0 copy-start
  67.9 0.0 copy-start.1
  67.9 6.1 %fusion.11 = f32[480,256]{1,0:T(8,128)S(1)} fusion(bf16[480,7168]{1,0:T(8,128)(2,1)} %reshape.28, bf16[1,7168,256]{2,1,0:T(8,128)(2,1)} %param.9), kind=kOutput, calls=%fused_computation.16 | convolution fusion | flops 1761607680 | bytes 11042816 | tf_op jit(solution)/shard_map/dot_general | solution.py:41
  74.0 0.0 copy-done
  74.0 0.9 copy-done.1
  74.9 0.0 copy-start.3
  74.9 2.7 multiply_convert_fusion.2
  77.6 0.0 copy-done.3
  77.6 4.8 %convolution_convert_fusion = bf16[480,7168]{1,0:T(8,128)(2,1)} fusion(bf16[480,256]{1,0:T(8,128)(2,1)S(1)} %get-tuple-element.12, bf16[1,256,7168]{2,1,0:T(8,128)(2,1)S(1)} %copy-done.3), kind=kOutput, calls=%fused_computation.1 | convolution fusion | flops 1765048320 | bytes 10797056 | tf_op jit(solution)/shard_map/dot_general | solution.py:45
  82.4 6.8 %reshape.25 = bf16[8,60,7168]{2,1,0:T(8,128)(2,1)} reshape(bf16[480,7168]{1,0:T(8,128)(2,1)} %convolution_convert_fusion) | data formatting | bytes 13762560 | tf_op jit(solution)/shard_map/reshape | solution.py:81
  89.2 0.0 reduce-scatter.3.cloned.1.call-update
  89.2 0.2 reduce-scatter.5.cloned.1.call-start
  89.5 0.5 collective-permute-start
  90.0 0.0 collective-permute-start.1
  90.0 12.9 %collective-permute-done = bf16[60,7168]{1,0:T(8,128)(2,1)S(1)} collective-permute-done((bf16[60,7168]{1,0:T(8,128)(2,1)S(1)}, bf16[60,7168]{1,0:T(8,128)(2,1)S(1)}, u32[]{:S(2)}, u32[]{:S(2)}) %collective-permute-start) | collective-permute-done | bytes 860192 | tf_op jit(solution)/shard_map/ppermute | solution.py:13
  102.9 2.5 collective-permute-start.2
  105.4 0.6 collective-permute-done.1
  106.0 0.0 copy-start.5
  106.0 2.6 collective-permute-start.3
  108.6 17.0 %collective-permute-done.2 = bf16[60,7168]{1,0:T(8,128)(2,1)S(1)} collective-permute-done((bf16[60,7168]{1,0:T(8,128)(2,1)S(1)}, bf16[60,7168]{1,0:T(8,128)(2,1)S(1)}, u32[]{:S(2)}, u32[]{:S(2)}) %collective-permute-start.2) | collective-permute-done | bytes 860192 | tf_op jit(solution)/shard_map/ppermute | solution.py:13
  125.6 0.0 copy-done.5
  125.6 0.0 copy-start.6
  125.6 2.5 collective-permute-start.4
  128.1 1.0 collective-permute-done.3
  129.1 0.0 copy-done.6
  129.1 3.4 %collective-permute-start.5 = (bf16[60,7168]{1,0:T(8,128)(2,1)}, bf16[60,7168]{1,0:T(8,128)(2,1)}, u32[]{:S(2)}, u32[]{:S(2)}) collective-permute-start(bf16[60,7168]{1,0:T(8,128)(2,1)} %collective-permute-done.3), channel_id=1, source_target_pairs={{0,7},{1,0},{2,1},{3,2},{4,3},{5,4},{6,5},{7,6},{8,15},{9,8},{10,9... | collective-permute-start | bytes 2580488 | tf_op jit(solution)/shard_map/ppermute | solution.py:16
  132.5 15.8 %collective-permute-done.4 = bf16[60,7168]{1,0:T(8,128)(2,1)} collective-permute-done((bf16[60,7168]{1,0:T(8,128)(2,1)S(1)}, bf16[60,7168]{1,0:T(8,128)(2,1)}, u32[]{:S(2)}, u32[]{:S(2)}) %collective-permute-start.4) | collective-permute-done | bytes 860192 | tf_op jit(solution)/shard_map/ppermute | solution.py:13
  148.4 2.6 collective-permute-start.6
  150.9 3.6 %broadcast_in_dim.45 = bf16[480,7168]{1,0:T(8,128)(2,1)} broadcast(bf16[]{:T(256)} %constant.61.clone.1), dimensions={} | broadcast | bytes 6881282 | tf_op jit(solution)/shard_map/broadcast_in_dim | solution.py:10
  154.5 4.5 %dynamic_update_slice.24 = bf16[480,7168]{1,0:T(8,128)(2,1)} dynamic-update-slice(bf16[480,7168]{1,0:T(8,128)(2,1)} %broadcast_in_dim.45, bf16[60,7168]{1,0:T(8,128)(2,1)S(1)} %get-tuple-element.15, s32[]{:T(128)S(6)} %select_n.74, s32[]{:T(128)} %constant.60.clone.1) | dynamic-update-slice | bytes 1720324 | tf_op jit(solution)/shard_map/dynamic_update_slice | solution.py:10
  159.0 4.5 %dynamic_update_slice.25 = bf16[480,7168]{1,0:T(8,128)(2,1)} dynamic-update-slice(bf16[480,7168]{1,0:T(8,128)(2,1)} %dynamic_update_slice.24, bf16[60,7168]{1,0:T(8,128)(2,1)S(1)} %collective-permute-done, s32[]{:T(128)S(6)} %select_n.76, s32[]{:T(128)} %constant.60.clone.1) | dynamic-update-slice | bytes 1720324 | tf_op jit(solution)/shard_map/dynamic_update_slice | solution.py:14
  163.5 4.8 %dynamic_update_slice.26 = bf16[480,7168]{1,0:T(8,128)(2,1)} dynamic-update-slice(bf16[480,7168]{1,0:T(8,128)(2,1)} %dynamic_update_slice.25, bf16[60,7168]{1,0:T(8,128)(2,1)} %copy-done.5, s32[]{:T(128)S(6)} %select_n.78, s32[]{:T(128)} %constant.60.clone.1) | dynamic-update-slice | bytes 1720324 | tf_op jit(solution)/shard_map/dynamic_update_slice | solution.py:17
  168.3 4.0 %dynamic_update_slice.27 = bf16[480,7168]{1,0:T(8,128)(2,1)} dynamic-update-slice(bf16[480,7168]{1,0:T(8,128)(2,1)} %dynamic_update_slice.26, bf16[60,7168]{1,0:T(8,128)(2,1)} %copy-done.6, s32[]{:T(128)S(6)} %select_n.80, s32[]{:T(128)} %constant.60.clone.1) | dynamic-update-slice | bytes 1720324 | tf_op jit(solution)/shard_map/dynamic_update_slice | solution.py:14
  172.3 4.8 %dynamic_update_slice.28 = bf16[480,7168]{1,0:T(8,128)(2,1)} dynamic-update-slice(bf16[480,7168]{1,0:T(8,128)(2,1)} %dynamic_update_slice.27, bf16[60,7168]{1,0:T(8,128)(2,1)} %collective-permute-done.3, s32[]{:T(128)S(6)} %select_n.82, s32[]{:T(128)} %constant.60.clone.1) | dynamic-update-slice | bytes 1720324 | tf_op jit(solution)/shard_map/dynamic_update_slice | solution.py:17
  177.1 4.8 %dynamic_update_slice.29 = bf16[480,7168]{1,0:T(8,128)(2,1)} dynamic-update-slice(bf16[480,7168]{1,0:T(8,128)(2,1)} %dynamic_update_slice.28, bf16[60,7168]{1,0:T(8,128)(2,1)} %collective-permute-done.4, s32[]{:T(128)S(6)} %select_n.84, s32[]{:T(128)} %constant.60.clone.1) | dynamic-update-slice | bytes 1720324 | tf_op jit(solution)/shard_map/dynamic_update_slice | solution.py:14
  181.9 0.0 collective-permute-done.5
  181.9 4.8 %dynamic_update_slice.30 = bf16[480,7168]{1,0:T(8,128)(2,1)} dynamic-update-slice(bf16[480,7168]{1,0:T(8,128)(2,1)} %dynamic_update_slice.29, bf16[60,7168]{1,0:T(8,128)(2,1)} %collective-permute-done.5, s32[]{:T(128)S(6)} %select_n.86, s32[]{:T(128)} %constant.60.clone.1) | dynamic-update-slice | bytes 1720324 | tf_op jit(solution)/shard_map/dynamic_update_slice | solution.py:17
  186.7 0.0 collective-permute-done.6
  186.7 4.8 %dynamic_update_slice.31 = bf16[480,7168]{1,0:T(8,128)(2,1)} dynamic-update-slice(bf16[480,7168]{1,0:T(8,128)(2,1)} %dynamic_update_slice.30, bf16[60,7168]{1,0:T(8,128)(2,1)} %collective-permute-done.6, s32[]{:T(128)S(6)} %select_n.88, s32[]{:T(128)} %constant.60.clone.1) | dynamic-update-slice | bytes 1720324 | tf_op jit(solution)/shard_map/dynamic_update_slice | solution.py:14
  191.4 0.0 copy-done.7
  191.4 6.2 %multiply_convert_fusion = (bf16[480,256]{1,0:T(8,128)(2,1)S(1)}, bf16[480,256]{1,0:T(8,128)(2,1)S(1)}) fusion(f32[480,256]{1,0:T(8,128)S(1)} %fusion.11, f32[480,256]{1,0:T(8,128)S(1)} %copy-done.7, bf16[480,7168]{1,0:T(8,128)(2,1)} %dynamic_update_slice.31, bf16[1,256,7168]{2,1,0:T(8,128)(2,1)} %param.11), kind=kOutput, calls=%fused_computation.21 | convolution fusion | flops 1763205120 | bytes 12025856 | tf_op jit(solution)/shard_map/dot_general | solution.py:29
  197.6 0.0 copy-done.4
  197.6 0.0 copy-start.2
  197.6 6.9 %fusion.9 = f32[480,7168]{1,0:T(8,128)} fusion(bf16[480,256]{1,0:T(8,128)(2,1)S(1)} %get-tuple-element.14, bf16[1,7168,256]{2,1,0:T(8,128)(2,1)S(1)} %copy-done.4), kind=kOutput, calls=%fused_computation.14 | convolution fusion | flops 1761607680 | bytes 17678336 | tf_op jit(solution)/shard_map/dot_general | solution.py:29
  204.6 0.0 copy-done.2
  204.6 9.8 %add_convert_fusion = bf16[480,7168]{1,0:T(8,128)(2,1)} fusion(f32[480,7168]{1,0:T(8,128)} %fusion.9, bf16[480,256]{1,0:T(8,128)(2,1)S(1)} %get-tuple-element.13, bf16[1,7168,256]{2,1,0:T(8,128)(2,1)S(1)} %copy-done.2), kind=kOutput, calls=%fused_computation | convolution fusion | flops 1768488960 | bytes 24559616 | tf_op jit(solution)/shard_map/dot_general | solution.py:29
  214.4 6.9 %reshape.26 = bf16[8,60,7168]{2,1,0:T(8,128)(2,1)} reshape(bf16[480,7168]{1,0:T(8,128)(2,1)} %add_convert_fusion) | data formatting | bytes 13762560 | tf_op jit(solution)/shard_map/reshape | solution.py:84
  221.2 0.0 reduce-scatter.5.cloned.1.call-update
  221.2 0.0 slice-start.1
  221.3 7.0 %fusion.2 = bf16[1,256,7168]{2,1,0:T(8,128)(2,1)} fusion(bf16[480,256]{1,0:T(8,128)(2,1)S(1)} %get-tuple-element.12, bf16[480,7168]{1,0:T(8,128)(2,1)} %dynamic_update_slice.31), kind=kOutput, calls=%fused_computation.7 | convolution fusion | flops 1763442688 | bytes 10797056 | tf_op jit(solution)/shard_map/dot_general | solution.py:35
  228.3 0.0 slice-done
  228.3 0.0 slice-done.1
  228.3 4.0 %fusion.1 = bf16[1,7168,256]{2,1,0:T(8,128)(2,1)} fusion(bf16[480,7168]{1,0:T(8,128)(2,1)S(1)} %bitcast.46, bf16[480,256]{1,0:T(8,128)(2,1)S(1)} %get-tuple-element.13), kind=kOutput, calls=%fused_computation.6 | convolution fusion | flops 1763442688 | bytes 10797056 | tf_op jit(solution)/shard_map/dot_general | solution.py:35
  232.3 4.0 %fusion = bf16[1,7168,256]{2,1,0:T(8,128)(2,1)} fusion(bf16[480,7168]{1,0:T(8,128)(2,1)S(1)} %bitcast.46, bf16[480,256]{1,0:T(8,128)(2,1)S(1)} %get-tuple-element.14), kind=kOutput, calls=%fused_computation.5 | convolution fusion | flops 1763442688 | bytes 10797056 | tf_op jit(solution)/shard_map/dot_general | solution.py:35
  236.4 35.6 %reduce-scatter.5.cloned.1.call-done = bf16[1,60,7168]{2,1,0:T(8,128)(2,1)} async-done(((bf16[8,60,7168]{2,1,0:T(8,128)(2,1)}), bf16[1,60,7168]{2,1,0:T(8,128)(2,1)}) %reduce-scatter.5.cloned.1.call-update) | async-done | bytes 860176 | tf_op jit(solution)/shard_map/reduce_scatter | solution.py:83
  (6 shorter events, 0.0 us)
Async XLA Ops:
  7.2 53.8 %all-gather.3.cloned.1.call-start = ((), (), s32[]{:S(2)}) async-start(), calls=%async_computation.4 | async-start | bytes 8257536 | tf_op jit(solution)/shard_map/all_gather | solution.py:74
  11.9 224.4 %reduce-scatter.3.cloned.1.call-start = ((), (), s32[]{:S(2)}) async-start(), calls=%async_computation.2 | async-start | bytes 8257536 | tf_op jit(solution)/shard_map/reduce_scatter | solution.py:80
  67.9 6.1 %copy-start = (bf16[480,7168]{1,0:T(8,128)(2,1)S(1)}, bf16[480,7168]{1,0:T(8,128)(2,1)}, u32[]{:S(2)}) copy-start(bf16[480,7168]{1,0:T(8,128)(2,1)} %reshape.28) | copy-start | bytes 20643844
  67.9 7.0 %copy-start.1 = (bf16[1,7168,256]{2,1,0:T(8,128)(2,1)S(1)}, bf16[1,7168,256]{2,1,0:T(8,128)(2,1)}, u32[]{:S(2)}) copy-start(bf16[1,7168,256]{2,1,0:T(8,128)(2,1)} %param.10) | copy-start | bytes 11010052
  74.9 2.7 copy-start.3
  89.2 182.8 %reduce-scatter.5.cloned.1.call-start = ((), (), s32[]{:S(2)}) async-start(), calls=%async_computation.3 | async-start | bytes 8257536 | tf_op jit(solution)/shard_map/reduce_scatter | solution.py:83
  89.5 13.5 %collective-permute-start = (bf16[60,7168]{1,0:T(8,128)(2,1)S(1)}, bf16[60,7168]{1,0:T(8,128)(2,1)S(1)}, u32[]{:S(2)}, u32[]{:S(2)}) collective-permute-start(bf16[60,7168]{1,0:T(8,128)(2,1)S(1)} %get-tuple-element.15), channel_id=1, source_target_pairs={{0,1},{1,2},{2,3},{3,4},{4,5},{5,6},{6,7},{7,0},{8,9},{9,10},{10,1... | collective-permute-start | bytes 2580488 | tf_op jit(solution)/shard_map/ppermute | solution.py:13
  90.0 16.0 %collective-permute-start.1 = (bf16[60,7168]{1,0:T(8,128)(2,1)S(1)}, bf16[60,7168]{1,0:T(8,128)(2,1)S(1)}, u32[]{:S(2)}, u32[]{:S(2)}) collective-permute-start(bf16[60,7168]{1,0:T(8,128)(2,1)S(1)} %get-tuple-element.15), channel_id=1, source_target_pairs={{0,7},{1,0},{2,1},{3,2},{4,3},{5,4},{6,5},{7,6},{8,15},{9,8},{10,9... | collective-permute-start | bytes 2580488 | tf_op jit(solution)/shard_map/ppermute | solution.py:16
  102.9 22.7 %collective-permute-start.2 = (bf16[60,7168]{1,0:T(8,128)(2,1)S(1)}, bf16[60,7168]{1,0:T(8,128)(2,1)S(1)}, u32[]{:S(2)}, u32[]{:S(2)}) collective-permute-start(bf16[60,7168]{1,0:T(8,128)(2,1)S(1)} %collective-permute-done), channel_id=1, source_target_pairs={{0,1},{1,2},{2,3},{3,4},{4,5},{5,6},{6,7},{7,0},{8,9},{9,10},{10,1... | collective-permute-start | bytes 2580488 | tf_op jit(solution)/shard_map/ppermute | solution.py:13
  106.0 19.6 %copy-start.5 = (bf16[60,7168]{1,0:T(8,128)(2,1)}, bf16[60,7168]{1,0:T(8,128)(2,1)S(1)}, u32[]{:S(2)}) copy-start(bf16[60,7168]{1,0:T(8,128)(2,1)S(1)} %collective-permute-done.1) | copy-start | bytes 2580484
  106.0 23.1 %collective-permute-start.3 = (bf16[60,7168]{1,0:T(8,128)(2,1)S(1)}, bf16[60,7168]{1,0:T(8,128)(2,1)}, u32[]{:S(2)}, u32[]{:S(2)}) collective-permute-start(bf16[60,7168]{1,0:T(8,128)(2,1)S(1)} %collective-permute-done.1), channel_id=1, source_target_pairs={{0,7},{1,0},{2,1},{3,2},{4,3},{5,4},{6,5},{7,6},{8,15},{9,8},{10,9... | collective-permute-start | bytes 2580488 | tf_op jit(solution)/shard_map/ppermute | solution.py:16
  125.6 3.5 %copy-start.6 = (bf16[60,7168]{1,0:T(8,128)(2,1)}, bf16[60,7168]{1,0:T(8,128)(2,1)S(1)}, u32[]{:S(2)}) copy-start(bf16[60,7168]{1,0:T(8,128)(2,1)S(1)} %collective-permute-done.2) | copy-start | bytes 2580484
  125.6 22.7 %collective-permute-start.4 = (bf16[60,7168]{1,0:T(8,128)(2,1)S(1)}, bf16[60,7168]{1,0:T(8,128)(2,1)}, u32[]{:S(2)}, u32[]{:S(2)}) collective-permute-start(bf16[60,7168]{1,0:T(8,128)(2,1)S(1)} %collective-permute-done.2), channel_id=1, source_target_pairs={{0,1},{1,2},{2,3},{3,4},{4,5},{5,6},{6,7},{7,0},{8,9},{9,10},{10,1... | collective-permute-start | bytes 2580488 | tf_op jit(solution)/shard_map/ppermute | solution.py:13
  129.1 52.8 %collective-permute-start.5 = (bf16[60,7168]{1,0:T(8,128)(2,1)}, bf16[60,7168]{1,0:T(8,128)(2,1)}, u32[]{:S(2)}, u32[]{:S(2)}) collective-permute-start(bf16[60,7168]{1,0:T(8,128)(2,1)} %collective-permute-done.3), channel_id=1, source_target_pairs={{0,7},{1,0},{2,1},{3,2},{4,3},{5,4},{6,5},{7,6},{8,15},{9,8},{10,9... | collective-permute-start | bytes 2580488 | tf_op jit(solution)/shard_map/ppermute | solution.py:16
  148.4 38.3 %collective-permute-start.6 = (bf16[60,7168]{1,0:T(8,128)(2,1)}, bf16[60,7168]{1,0:T(8,128)(2,1)}, u32[]{:S(2)}, u32[]{:S(2)}) collective-permute-start(bf16[60,7168]{1,0:T(8,128)(2,1)} %collective-permute-done.4), channel_id=1, source_target_pairs={{0,1},{1,2},{2,3},{3,4},{4,5},{5,6},{6,7},{7,0},{8,9},{9,10},{10,1... | collective-permute-start | bytes 2580488 | tf_op jit(solution)/shard_map/ppermute | solution.py:13
  159.0 32.5 %copy-start.7 = (f32[480,256]{1,0:T(8,128)S(1)}, f32[480,256]{1,0:T(8,128)}, u32[]{:S(2)}) copy-start(f32[480,256]{1,0:T(8,128)} %get-tuple-element.10) | copy-start | bytes 1474564
  191.4 6.2 %copy-start.4 = (bf16[1,7168,256]{2,1,0:T(8,128)(2,1)S(1)}, bf16[1,7168,256]{2,1,0:T(8,128)(2,1)}, u32[]{:S(2)}) copy-start(bf16[1,7168,256]{2,1,0:T(8,128)(2,1)} %param.9) | copy-start | bytes 11010052
  197.6 7.0 %copy-start.2 = (bf16[1,7168,256]{2,1,0:T(8,128)(2,1)S(1)}, bf16[1,7168,256]{2,1,0:T(8,128)(2,1)}, u32[]{:S(2)}) copy-start(bf16[1,7168,256]{2,1,0:T(8,128)(2,1)} %param.10) | copy-start | bytes 11010052
  221.2 7.1 %slice-start = ((s8[6881280]{0:T(1024)(128)(4,1)}), s8[2686976]{0:T(1024)(128)(4,1)S(1)}, s32[]{:S(2)}) async-start(s8[6881280]{0:T(1024)(128)(4,1)} %bitcast.45), calls=%async_computation.5 | async-start | bytes 5373952
  221.2 7.1 %slice-start.1 = ((s8[6881280]{0:T(1024)(128)(4,1)}), s8[4194304]{0:T(1024)(128)(4,1)S(1)}, s32[]{:S(2)}) async-start(s8[6881280]{0:T(1024)(128)(4,1)} %bitcast.45), calls=%async_computation.6 | async-start | bytes 8388608
Sparse Core Ops, SparseCore 0:
  12.0 48.8 all-gather.2
  89.4 69.1 reduce-scatter.2
  221.4 50.5 reduce-scatter.4
